TPU v7x, 512 devices: a whole 4x8x8 slice. The times are simulated.
512 devices in a mesh: gx: 16 (over y, core), gy: 32 (over x, z).
Axes of the slice: x: 4, y: 8, z: 8, core: 2. Of those that a mesh axis runs over, the one named last changes fastest.
Arguments:
- right_side: float32 [128, 262144], P('gx', 'gy'), may hold values from -6 to 6
- initial_guess: float32 [128, 262144], P('gx', 'gy'), may hold values from -1.2 to 1.2
- coefficients: float32 [5, 128, 16384], P(None, 'gx', 'gy'), may hold values from -1 to 2, as said below
Outputs:
- solution: float32 [128, 262144], P('gx', 'gy')
- residual: float32 [128, 262144], P('gx', 'gy')
Inputs may be any that keep to these rules, and one draw needn't show every extreme that they name: `coefficients`: component 0 is the diffusivity, within 0.5 to 2; components 1 to 3 the drift velocities along the three dimensions, within -1 to 1; component 4 the reaction rate, within 0.5 to 2.
All inputs are finite; a program needn't handle non-finite values.
Results may differ from a plain program's by a relative error of at most 0.0003.
Values sent between devices are 32-bit elements; how exact they have to be, the bound alone decides.
No kernel may reach another device: no remote copies, remote signals or barrier semaphores. Data moves between devices by JAX's collectives and lax.ppermute only.
A program may use at most 64 MiB of HBM per device.

v0:
```python
import jax
import jax.numpy as jnp
from jax import lax
from jax.sharding import PartitionSpec as P

NZ = 32
RHS = 16
STEPS = 3
SHIFT = 7.5
SCALE = 4.0


def extended(block, sides, width):
    for axis, dim in sides:
        count = lax.axis_size(axis)
        forward = [(i, i + 1) for i in range(count - 1)]
        backward = [(target, source) for source, target in forward]
        low = lax.ppermute(
            lax.slice_in_dim(block, block.shape[dim] - width, None, axis=dim), axis, forward
        )
        high = lax.ppermute(lax.slice_in_dim(block, 0, width, axis=dim), axis, backward)
        block = jnp.concatenate([low, block, high], axis=dim)
    return block


def operate(padded, coefs):
    diffusivity, drift_x, drift_y, drift_z, reaction = coefs
    center = padded[1:-1, 1:-1]
    x_plus = padded[2:, 1:-1]
    x_minus = padded[:-2, 1:-1]
    y_plus = padded[1:-1, 2:]
    y_minus = padded[1:-1, :-2]
    zero_rim = jnp.zeros(center.shape[:2] + (RHS,), center.dtype)
    z_plus = jnp.concatenate([center[:, :, RHS:], zero_rim], axis=2)
    z_minus = jnp.concatenate([zero_rim, center[:, :, :-RHS]], axis=2)
    beside = x_plus + x_minus + y_plus + y_minus + z_plus + z_minus
    drift = (
        drift_x * (x_plus - x_minus) + drift_y * (y_plus - y_minus) + drift_z * (z_plus - z_minus)
    )
    return (reaction + 6.0 * diffusivity) * center - diffusivity * beside + 0.5 * drift


def widen(table):
    return [jnp.repeat(table[:, :, i * NZ : (i + 1) * NZ], RHS, axis=2) for i in range(5)]


def combine_rhs(field, weights):
    lanes = jnp.kron(jnp.eye(128 // RHS, dtype=jnp.float32), weights)
    flat = field.reshape(-1, 128)
    return jnp.dot(flat, lanes, precision=lax.Precision.HIGHEST).reshape(field.shape)


def per_device(right_side, initial_guess, coefficients):
    rows_x = right_side.shape[0]
    rows_y = right_side.shape[1] // (NZ * RHS)
    width = NZ * RHS
    rhs_field = right_side.reshape(rows_x, rows_y, width)
    guess = initial_guess.reshape(rows_x, rows_y, width)
    coef_local = jnp.transpose(coefficients.reshape(5, rows_x, rows_y, NZ), (1, 2, 0, 3)).reshape(
        rows_x, rows_y, 5 * NZ
    )
    inner_coefs = widen(coef_local)
    guess_pad = extended(guess, (("gx", 0), ("gy", 1)), 1)
    initial_res = rhs_field - operate(guess_pad, inner_coefs)
    krylov = [initial_res]
    current = initial_res
    for step in range(STEPS):
        padded = extended(current, (("gx", 0), ("gy", 1)), 1)
        current = (operate(padded, inner_coefs) - SHIFT * current) / SCALE
        krylov.append(current)
    blocks = len(krylov)
    groups = 128 // RHS
    stacked = jnp.concatenate([v.reshape(-1, 128) for v in krylov], axis=1)
    products = jnp.dot(stacked.T, stacked, precision=lax.Precision.HIGHEST)
    products = products.reshape(blocks, groups, RHS, blocks, groups, RHS)
    diagonal = jnp.eye(groups, dtype=jnp.float32)[None, :, None, None, :, None]
    local_gram = jnp.sum(products * diagonal, axis=(1, 4)).reshape(blocks * RHS, blocks * RHS)
    gram = lax.psum(local_gram, ("gx", "gy"))
    shift_map = SHIFT * jnp.eye(blocks * RHS, STEPS * RHS, dtype=jnp.float32) + SCALE * jnp.eye(
        blocks * RHS, STEPS * RHS, k=-RHS, dtype=jnp.float32
    )
    normal = jnp.dot(
        shift_map.T,
        jnp.dot(gram, shift_map, precision=lax.Precision.HIGHEST),
        precision=lax.Precision.HIGHEST,
    )
    target = jnp.dot(shift_map.T, gram[:, :RHS], precision=lax.Precision.HIGHEST)
    factor = jnp.linalg.cholesky(normal)
    weights = jax.scipy.linalg.cho_solve((factor, True), target)
    solution = guess
    for step in range(STEPS):
        solution = solution + combine_rhs(krylov[step], weights[step * RHS : (step + 1) * RHS])
    update_pad = extended(solution, (("gx", 0), ("gy", 1)), 1)
    residual = rhs_field - operate(update_pad, inner_coefs)
    return (
        solution.reshape(rows_x, rows_y * NZ * RHS),
        residual.reshape(rows_x, rows_y * NZ * RHS),
    )


def solution(mesh):
    placed = (P("gx", "gy"), P("gx", "gy"), P(None, "gx", "gy"))
    return jax.shard_map(
        per_device,
        mesh=mesh,
        in_specs=placed,
        out_specs=(P("gx", "gy"), P("gx", "gy")),
        check_vma=False,
    )
```

profile of v0, /device:TPU:34, one launch (start us, length us, event | category | flops | bytes accessed | tf_op | source)
XLA Modules:
  0.0 240.8 jit_solution(5623281883208357478)
XLA Ops:
  0.6 1.3 slice_reduce_fusion.1
  1.9 1.9 collective-permute-start.1
  3.9 4.9 %collective-permute-start = (f32[1,16,512]{2,1,0:T(8,128)S(1)}, f32[1,16,512]{2,1,0:T(8,128)S(1)}, u32[]{:S(2)}, u32[]{:S(2)}) collective-permute-start(f32[1,16,512]{2,1,0:T(8,128)S(1)} %slice.224), channel_id=1, source_target_pairs={{32,0},{64,32},{96,64},{128,96},{160,128},{192,160},{224,192},{256... | collective-permute-start | bytes 98312 | tf_op jit(solution)/shard_map/ppermute | solution.py:21
  8.7 1.1 copy.35
  9.8 0.9 fusion.51
  10.7 1.0 reshape.149
  12.3 10.9 %collective-permute-start.2 = (f32[10,1,512]{2,1,0:T(1,128)S(1)}, f32[10,1,512]{2,1,0:T(1,128)S(1)}, u32[]{:S(2)}, u32[]{:S(2)}) collective-permute-start(f32[10,1,512]{2,1,0:T(1,128)S(1)} %get-tuple-element.16), channel_id=1, source_target_pairs={{1,0},{2,1},{3,2},{4,3},{5,4},{6,5},{7,6},{8,7},{9,8},{10,9},{11,1... | collective-permute-start | bytes 61448 | tf_op jit(solution)/shard_map/ppermute | solution.py:21
  23.3 1.9 collective-permute-start.3
  25.3 0.6 broadcast_in_dim.26
  25.9 1.6 reshape.151
  27.5 0.6 broadcast_in_dim.27
  28.1 1.6 reshape.152
  29.6 0.6 broadcast_in_dim.28
  30.3 1.6 reshape.154
  31.8 0.6 broadcast_in_dim.29
  32.4 1.6 reshape.155
  34.0 0.6 broadcast_in_dim.30
  34.6 1.6 reshape.156
  36.1 2.1 bitcast_subtract_fusion.1
  38.2 2.6 %collective-permute-start.4 = (f32[1,16,512]{2,1,0:T(8,128)S(1)}, f32[1,16,512]{2,1,0:T(8,128)S(1)}, u32[]{:S(2)}, u32[]{:S(2)}) collective-permute-start(f32[1,16,512]{2,1,0:T(8,128)S(1)} %get-tuple-element.31), channel_id=1, source_target_pairs={{32,0},{64,32},{96,64},{128,96},{160,128},{192,160},{224,192},{256... | collective-permute-start | bytes 98312 | tf_op jit(solution)/shard_map/ppermute | solution.py:21
  40.8 1.9 collective-permute-start.5
  42.8 4.5 %collective-permute-done.5 = f32[1,16,512]{2,1,0:T(8,128)S(1)} collective-permute-done((f32[1,16,512]{2,1,0:T(8,128)S(1)}, f32[1,16,512]{2,1,0:T(8,128)S(1)}, u32[]{:S(2)}, u32[]{:S(2)}) %collective-permute-start.5) | collective-permute-done | bytes 32800 | tf_op jit(solution)/shard_map/ppermute | solution.py:18
  47.3 5.8 %collective-permute-start.6 = (f32[10,1,512]{2,1,0:T(1,128)S(1)}, f32[10,1,512]{2,1,0:T(1,128)S(1)}, u32[]{:S(2)}, u32[]{:S(2)}) collective-permute-start(f32[10,1,512]{2,1,0:T(1,128)S(1)} %get-tuple-element.14), channel_id=1, source_target_pairs={{1,0},{2,1},{3,2},{4,3},{5,4},{6,5},{7,6},{8,7},{9,8},{10,9},{11,1... | collective-permute-start | bytes 61448 | tf_op jit(solution)/shard_map/ppermute | solution.py:21
  53.1 2.1 collective-permute-start.7
  55.3 5.5 %collective-permute-done.7 = f32[10,1,512]{2,1,0:T(1,128)S(1)} collective-permute-done((f32[10,1,512]{2,1,0:T(1,128)S(1)}, f32[10,1,512]{2,1,0:T(1,128)S(1)}, u32[]{:S(2)}, u32[]{:S(2)}) %collective-permute-start.7) | collective-permute-done | bytes 20512 | tf_op jit(solution)/shard_map/ppermute | solution.py:18
  60.9 0.3 broadcast_multiply_fusion.4
  61.2 1.9 collective-permute-start.8
  63.1 2.4 collective-permute-start.9
  65.5 4.0 %collective-permute-done.9 = f32[1,16,512]{2,1,0:T(8,128)S(1)} collective-permute-done((f32[1,16,512]{2,1,0:T(8,128)S(1)}, f32[1,16,512]{2,1,0:T(8,128)S(1)}, u32[]{:S(2)}, u32[]{:S(2)}) %collective-permute-start.9) | collective-permute-done | bytes 32800 | tf_op jit(solution)/shard_map/ppermute | solution.py:18
  69.6 1.9 collective-permute-start.10
  71.5 3.9 %collective-permute-start.11 = (f32[10,1,512]{2,1,0:T(1,128)S(1)}, f32[10,1,512]{2,1,0:T(1,128)S(1)}, u32[]{:S(2)}, u32[]{:S(2)}) collective-permute-start(f32[10,1,512]{2,1,0:T(1,128)S(1)} %get-tuple-element.13), channel_id=1, source_target_pairs={{0,1},{1,2},{2,3},{3,4},{4,5},{5,6},{6,7},{7,8},{8,9},{9,10},{10,1... | collective-permute-start | bytes 61448 | tf_op jit(solution)/shard_map/ppermute | solution.py:18
  75.6 3.7 %collective-permute-done.11 = f32[10,1,512]{2,1,0:T(1,128)S(1)} collective-permute-done((f32[10,1,512]{2,1,0:T(1,128)S(1)}, f32[10,1,512]{2,1,0:T(1,128)S(1)}, u32[]{:S(2)}, u32[]{:S(2)}) %collective-permute-start.11) | collective-permute-done | bytes 20512 | tf_op jit(solution)/shard_map/ppermute | solution.py:18
  79.3 0.3 broadcast_multiply_fusion.3
  79.6 1.9 collective-permute-start.12
  81.6 2.4 collective-permute-start.13
  84.1 4.0 %collective-permute-done.13 = f32[1,16,512]{2,1,0:T(8,128)S(1)} collective-permute-done((f32[1,16,512]{2,1,0:T(8,128)S(1)}, f32[1,16,512]{2,1,0:T(8,128)S(1)}, u32[]{:S(2)}, u32[]{:S(2)}) %collective-permute-start.13) | collective-permute-done | bytes 32800 | tf_op jit(solution)/shard_map/ppermute | solution.py:18
  88.1 1.9 collective-permute-start.14
  90.0 3.9 %collective-permute-start.15 = (f32[10,1,512]{2,1,0:T(1,128)S(1)}, f32[10,1,512]{2,1,0:T(1,128)S(1)}, u32[]{:S(2)}, u32[]{:S(2)}) collective-permute-start(f32[10,1,512]{2,1,0:T(1,128)S(1)} %get-tuple-element.11), channel_id=1, source_target_pairs={{0,1},{1,2},{2,3},{3,4},{4,5},{5,6},{6,7},{7,8},{8,9},{9,10},{10,1... | collective-permute-start | bytes 61448 | tf_op jit(solution)/shard_map/ppermute | solution.py:18
  94.1 3.7 %collective-permute-done.15 = f32[10,1,512]{2,1,0:T(1,128)S(1)} collective-permute-done((f32[10,1,512]{2,1,0:T(1,128)S(1)}, f32[10,1,512]{2,1,0:T(1,128)S(1)}, u32[]{:S(2)}, u32[]{:S(2)}) %collective-permute-start.15) | collective-permute-done | bytes 20512 | tf_op jit(solution)/shard_map/ppermute | solution.py:18
  97.8 0.3 subtract_multiply_fusion
  98.1 1.9 fusion
  100.0 4.9 %reshape.161 = f32[4,8,16,4,8,16]{5,4,3,2,1,0:T(8,128)} reshape(f32[512,512]{1,0:T(8,128)S(1)} %fusion) | data formatting | bytes 2097152 | tf_op jit(solution)/shard_map/reshape | solution.py:75
  104.9 4.8 %multiply_reduce_fusion = f32[4,16,4,16]{3,2,1,0:T(4,128)S(1)} fusion(f32[4,8,16,4,8,16]{5,4,3,2,1,0:T(8,128)} %reshape.161, f32[8,8]{1,0:T(8,128)S(1)} %fusion.31), kind=kLoop, calls=%fused_computation | loop fusion | flops 520192 | bytes 1065216 | tf_op jit(solution)/shard_map/reduce_sum | solution.py:77
  109.8 93.3 %psum.7 = f32[64,64]{1,0:T(8,128)S(1)} all-reduce(f32[64,64]{1,0:T(8,128)S(1)} %reshape.162), channel_id=1, replica_groups=mesh['gx'=16,'gy'=32] {'gx','gy'}, use_global_device_ids=true, to_apply=%region_1.0 | all-reduce | flops 4096 | bytes 32768 | tf_op jit(solution)/shard_map/psum | solution.py:78
  203.3 0.3 fusion.9
  203.6 0.3 fusion.11
  204.0 4.4 %cholesky.16 = f32[48,48]{1,0:T(8,128)S(1)} custom-call(f32[48,48]{1,0:T(8,128)S(1)} %fusion.18), custom_call_target="Cholesky" | custom-call | tf_op jit(solution)/shard_map/jit(cholesky)/cholesky | solution.py:88
  208.5 0.6 compare_reduce_fusion
  209.1 0.7 fusion.13
  209.8 3.7 %custom-call.10 = f32[1,48,48]{1,2,0:T(8,128)S(1)} custom-call(f32[1,48,48]{2,1,0:T(8,128)S(1)} %fusion.13), custom_call_target="InvertDiagBlocksLowerTriangular" | custom-call | tf_op jit(solution)/shard_map/jit(_cho_solve)/triangular_solve | solution.py:89
  213.4 0.2 fusion.16
  214.2 0.2 broadcast_multiply_fusion.2
  214.6 0.4 fusion.54
  215.3 0.4 fusion.55
  216.0 1.3 fusion.56
  217.7 4.1 %collective-permute-start.16 = (f32[1,16,512]{2,1,0:T(8,128)S(1)}, f32[1,16,512]{2,1,0:T(8,128)S(1)}, u32[]{:S(2)}, u32[]{:S(2)}) collective-permute-start(f32[1,16,512]{2,1,0:T(8,128)S(1)} %get-tuple-element.19), channel_id=1, source_target_pairs={{32,0},{64,32},{96,64},{128,96},{160,128},{192,160},{224,192},{256... | collective-permute-start | bytes 98312 | tf_op jit(solution)/shard_map/ppermute | solution.py:21
  221.8 1.9 collective-permute-start.17
  223.7 0.8 add_add_fusion.1
  224.5 3.8 %collective-permute-done.17 = f32[1,16,512]{2,1,0:T(8,128)S(1)} collective-permute-done((f32[1,16,512]{2,1,0:T(8,128)S(1)}, f32[1,16,512]{2,1,0:T(8,128)S(1)}, u32[]{:S(2)}, u32[]{:S(2)}) %collective-permute-start.17) | collective-permute-done | bytes 32800 | tf_op jit(solution)/shard_map/ppermute | solution.py:18
  228.3 3.4 %collective-permute-start.18 = (f32[10,1,512]{2,1,0:T(1,128)S(1)}, f32[10,1,512]{2,1,0:T(1,128)S(1)}, u32[]{:S(2)}, u32[]{:S(2)}) collective-permute-start(f32[10,1,512]{2,1,0:T(1,128)S(1)} %get-tuple-element.8), channel_id=1, source_target_pairs={{1,0},{2,1},{3,2},{4,3},{5,4},{6,5},{7,6},{8,7},{9,8},{10,9},{11,1... | collective-permute-start | bytes 61448 | tf_op jit(solution)/shard_map/ppermute | solution.py:21
  231.7 2.4 %collective-permute-start.19 = (f32[10,1,512]{2,1,0:T(1,128)S(1)}, f32[10,1,512]{2,1,0:T(1,128)S(1)}, u32[]{:S(2)}, u32[]{:S(2)}) collective-permute-start(f32[10,1,512]{2,1,0:T(1,128)S(1)} %get-tuple-element.9), channel_id=1, source_target_pairs={{0,1},{1,2},{2,3},{3,4},{4,5},{5,6},{6,7},{7,8},{8,9},{9,10},{10,1... | collective-permute-start | bytes 61448 | tf_op jit(solution)/shard_map/ppermute | solution.py:18
  234.3 5.2 %collective-permute-done.19 = f32[10,1,512]{2,1,0:T(1,128)S(1)} collective-permute-done((f32[10,1,512]{2,1,0:T(1,128)S(1)}, f32[10,1,512]{2,1,0:T(1,128)S(1)}, u32[]{:S(2)}, u32[]{:S(2)}) %collective-permute-start.19) | collective-permute-done | bytes 20512 | tf_op jit(solution)/shard_map/ppermute | solution.py:18
  239.5 0.5 fusion.8
  240.0 0.9 copy.25
  (71 shorter events, 3.5 us)
Async XLA Ops:
  0.6 11.5 %copy-start = (f32[8,8192]{1,0:T(8,128)S(1)}, f32[8,8192]{1,0:T(8,128)}, u32[]{:S(2)}) copy-start(f32[8,8192]{1,0:T(8,128)} %param.4) | copy-start | bytes 786436
  1.9 10.2 %collective-permute-start.1 = (f32[1,16,512]{2,1,0:T(8,128)S(1)}, f32[1,16,512]{2,1,0:T(8,128)S(1)}, u32[]{:S(2)}, u32[]{:S(2)}) collective-permute-start(f32[1,16,512]{2,1,0:T(8,128)S(1)} %slice.227), channel_id=1, source_target_pairs={{0,32},{32,64},{64,96},{96,128},{128,160},{160,192},{192,224},{224... | collective-permute-start | bytes 98312 | tf_op jit(solution)/shard_map/ppermute | solution.py:18
  3.9 8.4 %collective-permute-start = (f32[1,16,512]{2,1,0:T(8,128)S(1)}, f32[1,16,512]{2,1,0:T(8,128)S(1)}, u32[]{:S(2)}, u32[]{:S(2)}) collective-permute-start(f32[1,16,512]{2,1,0:T(8,128)S(1)} %slice.224), channel_id=1, source_target_pairs={{32,0},{64,32},{96,64},{128,96},{160,128},{192,160},{224,192},{256... | collective-permute-start | bytes 98312 | tf_op jit(solution)/shard_map/ppermute | solution.py:21
  9.8 15.5 %copy-start.2 = (f32[1,8,16,512]{3,2,1,0:T(8,128)}, f32[1,8,16,512]{3,2,1,0:T(8,128)S(1)}, u32[]{:S(2)}) copy-start(f32[1,8,16,512]{3,2,1,0:T(8,128)S(1)} %copy.35) | copy-start | bytes 786436
  12.3 15.2 %copy-start.5 = (f32[10,16,512]{2,1,0:T(8,128)}, f32[10,16,512]{2,1,0:T(8,128)S(1)}, u32[]{:S(2)}) copy-start(f32[10,16,512]{2,1,0:T(8,128)S(1)} %constant_dynamic-update-slice_fusion) | copy-start | bytes 983044
  12.3 23.8 %collective-permute-start.2 = (f32[10,1,512]{2,1,0:T(1,128)S(1)}, f32[10,1,512]{2,1,0:T(1,128)S(1)}, u32[]{:S(2)}, u32[]{:S(2)}) collective-permute-start(f32[10,1,512]{2,1,0:T(1,128)S(1)} %get-tuple-element.16), channel_id=1, source_target_pairs={{1,0},{2,1},{3,2},{4,3},{5,4},{6,5},{7,6},{8,7},{9,8},{10,9},{11,1... | collective-permute-start | bytes 61448 | tf_op jit(solution)/shard_map/ppermute | solution.py:21
  23.3 12.9 %collective-permute-start.3 = (f32[10,1,512]{2,1,0:T(1,128)S(1)}, f32[10,1,512]{2,1,0:T(1,128)S(1)}, u32[]{:S(2)}, u32[]{:S(2)}) collective-permute-start(f32[10,1,512]{2,1,0:T(1,128)S(1)} %get-tuple-element.17), channel_id=1, source_target_pairs={{0,1},{1,2},{2,3},{3,4},{4,5},{5,6},{6,7},{7,8},{8,9},{9,10},{10,1... | collective-permute-start | bytes 61448 | tf_op jit(solution)/shard_map/ppermute | solution.py:18
  38.2 4.5 %collective-permute-start.4 = (f32[1,16,512]{2,1,0:T(8,128)S(1)}, f32[1,16,512]{2,1,0:T(8,128)S(1)}, u32[]{:S(2)}, u32[]{:S(2)}) collective-permute-start(f32[1,16,512]{2,1,0:T(8,128)S(1)} %get-tuple-element.31), channel_id=1, source_target_pairs={{32,0},{64,32},{96,64},{128,96},{160,128},{192,160},{224,192},{256... | collective-permute-start | bytes 98312 | tf_op jit(solution)/shard_map/ppermute | solution.py:21
  40.8 6.4 %collective-permute-start.5 = (f32[1,16,512]{2,1,0:T(8,128)S(1)}, f32[1,16,512]{2,1,0:T(8,128)S(1)}, u32[]{:S(2)}, u32[]{:S(2)}) collective-permute-start(f32[1,16,512]{2,1,0:T(8,128)S(1)} %get-tuple-element.30), channel_id=1, source_target_pairs={{0,32},{32,64},{64,96},{96,128},{128,160},{160,192},{192,224},{224... | collective-permute-start | bytes 98312 | tf_op jit(solution)/shard_map/ppermute | solution.py:18
  47.3 8.0 %collective-permute-start.6 = (f32[10,1,512]{2,1,0:T(1,128)S(1)}, f32[10,1,512]{2,1,0:T(1,128)S(1)}, u32[]{:S(2)}, u32[]{:S(2)}) collective-permute-start(f32[10,1,512]{2,1,0:T(1,128)S(1)} %get-tuple-element.14), channel_id=1, source_target_pairs={{1,0},{2,1},{3,2},{4,3},{5,4},{6,5},{7,6},{8,7},{9,8},{10,9},{11,1... | collective-permute-start | bytes 61448 | tf_op jit(solution)/shard_map/ppermute | solution.py:21
  53.1 7.8 %collective-permute-start.7 = (f32[10,1,512]{2,1,0:T(1,128)S(1)}, f32[10,1,512]{2,1,0:T(1,128)S(1)}, u32[]{:S(2)}, u32[]{:S(2)}) collective-permute-start(f32[10,1,512]{2,1,0:T(1,128)S(1)} %get-tuple-element.15), channel_id=1, source_target_pairs={{0,1},{1,2},{2,3},{3,4},{4,5},{5,6},{6,7},{7,8},{8,9},{9,10},{10,1... | collective-permute-start | bytes 61448 | tf_op jit(solution)/shard_map/ppermute | solution.py:18
  61.2 4.4 %collective-permute-start.8 = (f32[1,16,512]{2,1,0:T(8,128)S(1)}, f32[1,16,512]{2,1,0:T(8,128)S(1)}, u32[]{:S(2)}, u32[]{:S(2)}) collective-permute-start(f32[1,16,512]{2,1,0:T(8,128)S(1)} %get-tuple-element.27), channel_id=1, source_target_pairs={{32,0},{64,32},{96,64},{128,96},{160,128},{192,160},{224,192},{256... | collective-permute-start | bytes 98312 | tf_op jit(solution)/shard_map/ppermute | solution.py:21
  63.1 6.4 %collective-permute-start.9 = (f32[1,16,512]{2,1,0:T(8,128)S(1)}, f32[1,16,512]{2,1,0:T(8,128)S(1)}, u32[]{:S(2)}, u32[]{:S(2)}) collective-permute-start(f32[1,16,512]{2,1,0:T(8,128)S(1)} %get-tuple-element.26), channel_id=1, source_target_pairs={{0,32},{32,64},{64,96},{96,128},{128,160},{160,192},{192,224},{224... | collective-permute-start | bytes 98312 | tf_op jit(solution)/shard_map/ppermute | solution.py:18
  69.6 6.0 %collective-permute-start.10 = (f32[10,1,512]{2,1,0:T(1,128)S(1)}, f32[10,1,512]{2,1,0:T(1,128)S(1)}, u32[]{:S(2)}, u32[]{:S(2)}) collective-permute-start(f32[10,1,512]{2,1,0:T(1,128)S(1)} %get-tuple-element.12), channel_id=1, source_target_pairs={{1,0},{2,1},{3,2},{4,3},{5,4},{6,5},{7,6},{8,7},{9,8},{10,9},{11,1... | collective-permute-start | bytes 61448 | tf_op jit(solution)/shard_map/ppermute | solution.py:21
  71.5 7.8 %collective-permute-start.11 = (f32[10,1,512]{2,1,0:T(1,128)S(1)}, f32[10,1,512]{2,1,0:T(1,128)S(1)}, u32[]{:S(2)}, u32[]{:S(2)}) collective-permute-start(f32[10,1,512]{2,1,0:T(1,128)S(1)} %get-tuple-element.13), channel_id=1, source_target_pairs={{0,1},{1,2},{2,3},{3,4},{4,5},{5,6},{6,7},{7,8},{8,9},{9,10},{10,1... | collective-permute-start | bytes 61448 | tf_op jit(solution)/shard_map/ppermute | solution.py:18
  79.6 4.4 %collective-permute-start.12 = (f32[1,16,512]{2,1,0:T(8,128)S(1)}, f32[1,16,512]{2,1,0:T(8,128)S(1)}, u32[]{:S(2)}, u32[]{:S(2)}) collective-permute-start(f32[1,16,512]{2,1,0:T(8,128)S(1)} %get-tuple-element.23), channel_id=1, source_target_pairs={{32,0},{64,32},{96,64},{128,96},{160,128},{192,160},{224,192},{256... | collective-permute-start | bytes 98312 | tf_op jit(solution)/shard_map/ppermute | solution.py:21
  81.6 6.4 %collective-permute-start.13 = (f32[1,16,512]{2,1,0:T(8,128)S(1)}, f32[1,16,512]{2,1,0:T(8,128)S(1)}, u32[]{:S(2)}, u32[]{:S(2)}) collective-permute-start(f32[1,16,512]{2,1,0:T(8,128)S(1)} %get-tuple-element.22), channel_id=1, source_target_pairs={{0,32},{32,64},{64,96},{96,128},{128,160},{160,192},{192,224},{224... | collective-permute-start | bytes 98312 | tf_op jit(solution)/shard_map/ppermute | solution.py:18
  88.1 6.0 %collective-permute-start.14 = (f32[10,1,512]{2,1,0:T(1,128)S(1)}, f32[10,1,512]{2,1,0:T(1,128)S(1)}, u32[]{:S(2)}, u32[]{:S(2)}) collective-permute-start(f32[10,1,512]{2,1,0:T(1,128)S(1)} %get-tuple-element.10), channel_id=1, source_target_pairs={{1,0},{2,1},{3,2},{4,3},{5,4},{6,5},{7,6},{8,7},{9,8},{10,9},{11,1... | collective-permute-start | bytes 61448 | tf_op jit(solution)/shard_map/ppermute | solution.py:21
  90.0 7.8 %collective-permute-start.15 = (f32[10,1,512]{2,1,0:T(1,128)S(1)}, f32[10,1,512]{2,1,0:T(1,128)S(1)}, u32[]{:S(2)}, u32[]{:S(2)}) collective-permute-start(f32[10,1,512]{2,1,0:T(1,128)S(1)} %get-tuple-element.11), channel_id=1, source_target_pairs={{0,1},{1,2},{2,3},{3,4},{4,5},{5,6},{6,7},{7,8},{8,9},{9,10},{10,1... | collective-permute-start | bytes 61448 | tf_op jit(solution)/shard_map/ppermute | solution.py:18
  94.1 5.9 %copy-start.3 = (f32[512,128]{1,0:T(8,128)}, f32[512,128]{1,0:T(8,128)S(1)}, u32[]{:S(2)}) copy-start(f32[512,128]{1,0:T(8,128)S(1)} %reshape.159) | copy-start | bytes 786436
  215.1 2.3 copy-start.1
  217.4 22.1 %copy-start.4 = (f32[8,8192]{1,0:T(8,128)S(1)}, f32[8,8192]{1,0:T(8,128)}, u32[]{:S(2)}) copy-start(f32[8,8192]{1,0:T(8,128)} %param.3) | copy-start | bytes 786436
  217.7 6.8 %collective-permute-start.16 = (f32[1,16,512]{2,1,0:T(8,128)S(1)}, f32[1,16,512]{2,1,0:T(8,128)S(1)}, u32[]{:S(2)}, u32[]{:S(2)}) collective-permute-start(f32[1,16,512]{2,1,0:T(8,128)S(1)} %get-tuple-element.19), channel_id=1, source_target_pairs={{32,0},{64,32},{96,64},{128,96},{160,128},{192,160},{224,192},{256... | collective-permute-start | bytes 98312 | tf_op jit(solution)/shard_map/ppermute | solution.py:21
  221.8 6.4 %collective-permute-start.17 = (f32[1,16,512]{2,1,0:T(8,128)S(1)}, f32[1,16,512]{2,1,0:T(8,128)S(1)}, u32[]{:S(2)}, u32[]{:S(2)}) collective-permute-start(f32[1,16,512]{2,1,0:T(8,128)S(1)} %get-tuple-element.18), channel_id=1, source_target_pairs={{0,32},{32,64},{64,96},{96,128},{128,160},{160,192},{192,224},{224... | collective-permute-start | bytes 98312 | tf_op jit(solution)/shard_map/ppermute | solution.py:18
  228.3 6.0 %collective-permute-start.18 = (f32[10,1,512]{2,1,0:T(1,128)S(1)}, f32[10,1,512]{2,1,0:T(1,128)S(1)}, u32[]{:S(2)}, u32[]{:S(2)}) collective-permute-start(f32[10,1,512]{2,1,0:T(1,128)S(1)} %get-tuple-element.8), channel_id=1, source_target_pairs={{1,0},{2,1},{3,2},{4,3},{5,4},{6,5},{7,6},{8,7},{9,8},{10,9},{11,1... | collective-permute-start | bytes 61448 | tf_op jit(solution)/shard_map/ppermute | solution.py:21
  231.7 7.8 %collective-permute-start.19 = (f32[10,1,512]{2,1,0:T(1,128)S(1)}, f32[10,1,512]{2,1,0:T(1,128)S(1)}, u32[]{:S(2)}, u32[]{:S(2)}) collective-permute-start(f32[10,1,512]{2,1,0:T(1,128)S(1)} %get-tuple-element.9), channel_id=1, source_target_pairs={{0,1},{1,2},{2,3},{3,4},{4,5},{5,6},{6,7},{7,8},{8,9},{9,10},{10,1... | collective-permute-start | bytes 61448 | tf_op jit(solution)/shard_map/ppermute | solution.py:18
where the time goes:
time: 242 us; the launch traced here: 241 us
  blocking collectives  93.3 us (39%)
  starting transfers between devices  64.2 us (27%)
  waiting for transfers between devices  34.4 us (14%)
  local copies, waits for them, and re-layouts  23.5 us (10%)
  other arithmetic  19 us (8%)
  matrix products  5.16 us (2%)
    psum x1, blocking collectives, per_device(): gram = lax.psum(local_gram, ('gx', 'gy'))  93.3 us
    ppermute x10, starting transfers between devices, extended(): lax.ppermute(lax.slice_in_dim(block, 0, width, axis=dim), axis, backward)  39.3 us
    ppermute x10, waiting for transfers between devices, extended(): lax.ppermute(lax.slice_in_dim(block, block.shape[dim] - width, None, axis...  34.3 us
    ppermute x10, starting transfers between devices, extended(): lax.ppermute(lax.slice_in_dim(block, block.shape[dim] - width, None, axis...  24.9 us
    reshape x5, local copies, waits for them, and re-layouts, widen(): jnp.repeat(table[:, :, i * NZ:(i + 1) * NZ], RHS, axis=2)  7.77 us
    another operation x3, other arithmetic, per_device(): factor = jnp.linalg.cholesky(normal)  5.05 us
    reshape x1, local copies, waits for them, and re-layouts, per_device(): products = products.reshape(blocks, groups, RHS, blocks, groups, RHS)  4.93 us
  transfers between devices with their start and end apart: 20, of which 8 were waited for; matrix products, arithmetic and copies ran while one was open for 7% of the time, Pallas kernels for 0%

commit v1 on v0

--- a/solution.py
+++ b/solution.py
@@ -75,7 +75,7 @@
     products = products.reshape(blocks, groups, RHS, blocks, groups, RHS)
     diagonal = jnp.eye(groups, dtype=jnp.float32)[None, :, None, None, :, None]
     local_gram = jnp.sum(products * diagonal, axis=(1, 4)).reshape(blocks * RHS, blocks * RHS)
-    gram = lax.psum(local_gram, ("gx", "gy"))
+    gram = jnp.sum(lax.all_gather(local_gram, axis_name=("gx", "gy")), axis=0)
     shift_map = SHIFT * jnp.eye(blocks * RHS, STEPS * RHS, dtype=jnp.float32) + SCALE * jnp.eye(
         blocks * RHS, STEPS * RHS, k=-RHS, dtype=jnp.float32
     )

time: 242 us -> 305 us (1.26)
  waiting for transfers between devices: 34.4 us -> 163 us
  blocking collectives: 93.3 us -> 0 us
  between operations: 1.34 us -> 14.7 us
  other arithmetic: 19 us -> 28 us
    all_gather x0 -> x1, waiting for transfers between devices: none -> 129 us  [per_device(): gram = jnp.sum(lax.all_gather(local_gram, axis_name=('gx', 'gy')), axis=0)]
    psum x1 -> x0, blocking collectives: 93.3 us -> none  [per_device(): gram = lax.psum(local_gram, ('gx', 'gy'))]
    reduce_sum x0 -> x1, other arithmetic: none -> 6.94 us  [per_device(): gram = jnp.sum(lax.all_gather(local_gram, axis_name=('gx', 'gy')), axis=0)]
  transfers between devices with their start and end apart: 20 -> 21, of which waited for: 8 -> 9; matrix products, arithmetic and copies ran while one was open for 7% -> 6% of each run, Pallas kernels for 0% -> 0%
where the time goes in v1:
time: 305 us; the launch traced here: 303 us
  waiting for transfers between devices  163 us (53%)
  starting transfers between devices  64.5 us (21%)
  other arithmetic  28 us (9%)
  local copies, waits for them, and re-layouts  26.4 us (9%)
  between operations  14.7 us (5%)
  matrix products  6.93 us (2%)
    all_gather x1, waiting for transfers between devices, per_device(): gram = jnp.sum(lax.all_gather(local_gram, axis_name=('gx', 'gy')), axis=0)  129 us
    ppermute x10, starting transfers between devices, extended(): lax.ppermute(lax.slice_in_dim(block, 0, width, axis=dim), axis, backward)  39.7 us
    ppermute x10, waiting for transfers between devices, extended(): lax.ppermute(lax.slice_in_dim(block, block.shape[dim] - width, None, axis...  34.3 us
    ppermute x10, starting transfers between devices, extended(): lax.ppermute(lax.slice_in_dim(block, block.shape[dim] - width, None, axis...  24.8 us
    reshape x5, local copies, waits for them, and re-layouts, widen(): jnp.repeat(table[:, :, i * NZ:(i + 1) * NZ], RHS, axis=2)  7.77 us
    reduce_sum x1, other arithmetic, per_device(): gram = jnp.sum(lax.all_gather(local_gram, axis_name=('gx', 'gy')), axis=0)  6.94 us
  transfers between devices with their start and end apart: 21, of which 9 were waited for; matrix products, arithmetic and copies ran while one was open for 6% of the time, Pallas kernels for 0%

profile of v1, /device:TPU:34, one launch (start us, length us, event | category | flops | bytes accessed | tf_op | source)
XLA Modules:
  0.0 303.5 jit_solution(8978388759258726462)
XLA Ops:
  7.2 1.2 slice_reduce_fusion.1
  8.4 1.9 collective-permute-start.1
  10.4 4.9 %collective-permute-start = (f32[1,16,512]{2,1,0:T(8,128)S(1)}, f32[1,16,512]{2,1,0:T(8,128)S(1)}, u32[]{:S(2)}, u32[]{:S(2)}) collective-permute-start(f32[1,16,512]{2,1,0:T(8,128)S(1)} %slice.224), channel_id=1, source_target_pairs={{32,0},{64,32},{96,64},{128,96},{160,128},{192,160},{224,192},{256... | collective-permute-start | bytes 98312 | tf_op jit(solution)/shard_map/ppermute | solution.py:21
  15.2 1.1 copy.40
  16.3 0.9 fusion.51
  17.3 1.0 reshape.146
  18.6 1.1 constant_dynamic-update-slice_fusion.1
  19.8 0.7 fusion.42
  20.5 10.9 %collective-permute-start.2 = (f32[10,1,512]{2,1,0:T(1,128)}, f32[10,1,512]{2,1,0:T(1,128)}, u32[]{:S(2)}, u32[]{:S(2)}) collective-permute-start(f32[10,1,512]{2,1,0:T(1,128)} %get-tuple-element.16), channel_id=1, source_target_pairs={{1,0},{2,1},{3,2},{4,3},{5,4},{6,5},{7,6},{8,7},{9,8},{10,9},{11,1... | collective-permute-start | bytes 61448 | tf_op jit(solution)/shard_map/ppermute | solution.py:21
  31.4 1.9 collective-permute-start.3
  33.5 0.6 broadcast_in_dim.26
  34.1 1.6 reshape.148
  35.6 0.6 broadcast_in_dim.27
  36.3 1.6 reshape.149
  37.8 0.6 broadcast_in_dim.28
  38.4 1.6 reshape.151
  40.0 0.6 broadcast_in_dim.29
  40.6 1.6 reshape.152
  42.1 0.6 broadcast_in_dim.30
  42.7 1.6 reshape.153
  44.3 2.1 bitcast_subtract_fusion.1
  46.4 1.9 collective-permute-start.4
  48.3 2.4 collective-permute-start.5
  50.7 4.0 %collective-permute-done.5 = f32[1,16,512]{2,1,0:T(8,128)S(1)} collective-permute-done((f32[1,16,512]{2,1,0:T(8,128)S(1)}, f32[1,16,512]{2,1,0:T(8,128)S(1)}, u32[]{:S(2)}, u32[]{:S(2)}) %collective-permute-start.5) | collective-permute-done | bytes 32800 | tf_op jit(solution)/shard_map/ppermute | solution.py:18
  54.8 6.0 %collective-permute-start.6 = (f32[10,1,512]{2,1,0:T(1,128)S(1)}, f32[10,1,512]{2,1,0:T(1,128)S(1)}, u32[]{:S(2)}, u32[]{:S(2)}) collective-permute-start(f32[10,1,512]{2,1,0:T(1,128)S(1)} %get-tuple-element.14), channel_id=1, source_target_pairs={{1,0},{2,1},{3,2},{4,3},{5,4},{6,5},{7,6},{8,7},{9,8},{10,9},{11,1... | collective-permute-start | bytes 61448 | tf_op jit(solution)/shard_map/ppermute | solution.py:21
  60.8 2.1 collective-permute-start.7
  63.1 5.5 %collective-permute-done.7 = f32[10,1,512]{2,1,0:T(1,128)S(1)} collective-permute-done((f32[10,1,512]{2,1,0:T(1,128)S(1)}, f32[10,1,512]{2,1,0:T(1,128)S(1)}, u32[]{:S(2)}, u32[]{:S(2)}) %collective-permute-start.7) | collective-permute-done | bytes 20512 | tf_op jit(solution)/shard_map/ppermute | solution.py:18
  68.9 1.9 collective-permute-start.8
  70.9 2.4 collective-permute-start.9
  73.3 4.0 %collective-permute-done.9 = f32[1,16,512]{2,1,0:T(8,128)S(1)} collective-permute-done((f32[1,16,512]{2,1,0:T(8,128)S(1)}, f32[1,16,512]{2,1,0:T(8,128)S(1)}, u32[]{:S(2)}, u32[]{:S(2)}) %collective-permute-start.9) | collective-permute-done | bytes 32800 | tf_op jit(solution)/shard_map/ppermute | solution.py:18
  77.4 1.9 collective-permute-start.10
  79.3 3.9 %collective-permute-start.11 = (f32[10,1,512]{2,1,0:T(1,128)S(1)}, f32[10,1,512]{2,1,0:T(1,128)S(1)}, u32[]{:S(2)}, u32[]{:S(2)}) collective-permute-start(f32[10,1,512]{2,1,0:T(1,128)S(1)} %get-tuple-element.13), channel_id=1, source_target_pairs={{0,1},{1,2},{2,3},{3,4},{4,5},{5,6},{6,7},{7,8},{8,9},{9,10},{10,1... | collective-permute-start | bytes 61448 | tf_op jit(solution)/shard_map/ppermute | solution.py:18
  83.4 3.7 %collective-permute-done.11 = f32[10,1,512]{2,1,0:T(1,128)S(1)} collective-permute-done((f32[10,1,512]{2,1,0:T(1,128)S(1)}, f32[10,1,512]{2,1,0:T(1,128)S(1)}, u32[]{:S(2)}, u32[]{:S(2)}) %collective-permute-start.11) | collective-permute-done | bytes 20512 | tf_op jit(solution)/shard_map/ppermute | solution.py:18
  87.1 0.3 broadcast_multiply_fusion.3
  87.4 1.9 collective-permute-start.12
  89.3 2.4 collective-permute-start.13
  91.9 3.9 %collective-permute-done.13 = f32[1,16,512]{2,1,0:T(8,128)S(1)} collective-permute-done((f32[1,16,512]{2,1,0:T(8,128)S(1)}, f32[1,16,512]{2,1,0:T(8,128)S(1)}, u32[]{:S(2)}, u32[]{:S(2)}) %collective-permute-start.13) | collective-permute-done | bytes 32800 | tf_op jit(solution)/shard_map/ppermute | solution.py:18
  95.8 1.9 collective-permute-start.14
  97.8 3.9 %collective-permute-start.15 = (f32[10,1,512]{2,1,0:T(1,128)S(1)}, f32[10,1,512]{2,1,0:T(1,128)S(1)}, u32[]{:S(2)}, u32[]{:S(2)}) collective-permute-start(f32[10,1,512]{2,1,0:T(1,128)S(1)} %get-tuple-element.11), channel_id=1, source_target_pairs={{0,1},{1,2},{2,3},{3,4},{4,5},{5,6},{6,7},{7,8},{8,9},{9,10},{10,1... | collective-permute-start | bytes 61448 | tf_op jit(solution)/shard_map/ppermute | solution.py:18
  101.9 3.7 %collective-permute-done.15 = f32[10,1,512]{2,1,0:T(1,128)S(1)} collective-permute-done((f32[10,1,512]{2,1,0:T(1,128)S(1)}, f32[10,1,512]{2,1,0:T(1,128)S(1)}, u32[]{:S(2)}, u32[]{:S(2)}) %collective-permute-start.15) | collective-permute-done | bytes 20512 | tf_op jit(solution)/shard_map/ppermute | solution.py:18
  105.9 1.9 fusion
  107.8 4.9 %reshape.158 = f32[4,8,16,4,8,16]{5,4,3,2,1,0:T(8,128)} reshape(f32[512,512]{1,0:T(8,128)S(1)} %fusion) | data formatting | bytes 2097152 | tf_op jit(solution)/shard_map/reshape | solution.py:75
  112.7 4.8 %multiply_reduce_fusion = f32[4,16,4,16]{3,2,1,0:T(4,128)S(1)} fusion(f32[4,8,16,4,8,16]{5,4,3,2,1,0:T(8,128)} %reshape.158, f32[8,8]{1,0:T(8,128)S(1)} %fusion.31), kind=kLoop, calls=%fused_computation | loop fusion | flops 520192 | bytes 1065216 | tf_op jit(solution)/shard_map/reduce_sum | solution.py:77
  117.5 0.7 all_gather_reshape.3
  118.2 128.6 %all-gather.2.cloned.1.call-done = f32[512,64,64]{2,1,0:T(8,128)} async-done(((f32[1,64,64]{2,1,0:T(8,128)}), f32[512,64,64]{2,1,0:T(8,128)}) %all-gather.2.cloned.1.call-update) | async-done | bytes 8388624 | tf_op jit(solution)/shard_map/all_gather | solution.py:78
  246.8 6.9 %reduce_sum.19 = f32[64,64]{1,0:T(8,128)S(1)} reduce(f32[512,64,64]{2,1,0:T(8,128)} %all-gather.2.cloned.1.call-done, f32[]{:T(128)} %constant.62.clone.1), dimensions={0}, to_apply=%region_1.0 | reduce | flops 2093056 | bytes 8404996 | tf_op jit(solution)/shard_map/reduce_sum | solution.py:78
  254.7 4.4 %cholesky.16 = f32[48,48]{1,0:T(8,128)S(1)} custom-call(f32[48,48]{1,0:T(8,128)S(1)} %fusion.18), custom_call_target="Cholesky" | custom-call | tf_op jit(solution)/shard_map/jit(cholesky)/cholesky | solution.py:88
  259.1 0.7 compare_reduce_fusion
  259.9 0.7 fusion.13
  260.6 3.7 %custom-call.10 = f32[1,48,48]{1,2,0:T(8,128)S(1)} custom-call(f32[1,48,48]{2,1,0:T(8,128)S(1)} %fusion.13), custom_call_target="InvertDiagBlocksLowerTriangular" | custom-call | tf_op jit(solution)/shard_map/jit(_cho_solve)/triangular_solve | solution.py:89
  265.3 1.3 fusion.54
  266.9 1.3 fusion.55
  268.2 0.7 reshape.163
  269.2 1.3 fusion.56
  270.6 1.2 add_add_fusion
  271.8 3.4 %collective-permute-start.16 = (f32[1,16,512]{2,1,0:T(8,128)S(1)}, f32[1,16,512]{2,1,0:T(8,128)S(1)}, u32[]{:S(2)}, u32[]{:S(2)}) collective-permute-start(f32[1,16,512]{2,1,0:T(8,128)S(1)} %get-tuple-element.19), channel_id=1, source_target_pairs={{32,0},{64,32},{96,64},{128,96},{160,128},{192,160},{224,192},{256... | collective-permute-start | bytes 98312 | tf_op jit(solution)/shard_map/ppermute | solution.py:21
  275.2 1.9 collective-permute-start.17
  277.1 0.8 add_add_fusion.1
  277.9 3.8 %collective-permute-done.17 = f32[1,16,512]{2,1,0:T(8,128)S(1)} collective-permute-done((f32[1,16,512]{2,1,0:T(8,128)S(1)}, f32[1,16,512]{2,1,0:T(8,128)S(1)}, u32[]{:S(2)}, u32[]{:S(2)}) %collective-permute-start.17) | collective-permute-done | bytes 32800 | tf_op jit(solution)/shard_map/ppermute | solution.py:18
  281.7 4.9 %collective-permute-start.18 = (f32[10,1,512]{2,1,0:T(1,128)S(1)}, f32[10,1,512]{2,1,0:T(1,128)S(1)}, u32[]{:S(2)}, u32[]{:S(2)}) collective-permute-start(f32[10,1,512]{2,1,0:T(1,128)S(1)} %get-tuple-element.8), channel_id=1, source_target_pairs={{1,0},{2,1},{3,2},{4,3},{5,4},{6,5},{7,6},{8,7},{9,8},{10,9},{11,1... | collective-permute-start | bytes 61448 | tf_op jit(solution)/shard_map/ppermute | solution.py:21
  286.6 1.9 collective-permute-start.19
  288.7 5.7 %collective-permute-done.19 = f32[10,1,512]{2,1,0:T(1,128)S(1)} collective-permute-done((f32[10,1,512]{2,1,0:T(1,128)S(1)}, f32[10,1,512]{2,1,0:T(1,128)S(1)}, u32[]{:S(2)}, u32[]{:S(2)}) %collective-permute-start.19) | collective-permute-done | bytes 20512 | tf_op jit(solution)/shard_map/ppermute | solution.py:18
  294.4 1.4 fusion.8
  295.8 0.9 copy.30
  (74 shorter events, 4.6 us)
Async XLA Ops:
  7.2 239.7 %all-gather.2.cloned.1.call-start = ((), (), s32[]{:S(2)}) async-start(), calls=%async_computation | async-start | bytes 16809984 | tf_op jit(solution)/shard_map/all_gather | solution.py:78
  8.4 10.2 %collective-permute-start.1 = (f32[1,16,512]{2,1,0:T(8,128)S(1)}, f32[1,16,512]{2,1,0:T(8,128)S(1)}, u32[]{:S(2)}, u32[]{:S(2)}) collective-permute-start(f32[1,16,512]{2,1,0:T(8,128)S(1)} %slice.227), channel_id=1, source_target_pairs={{0,32},{32,64},{64,96},{96,128},{128,160},{160,192},{192,224},{224... | collective-permute-start | bytes 98312 | tf_op jit(solution)/shard_map/ppermute | solution.py:18
  10.4 9.4 %collective-permute-start = (f32[1,16,512]{2,1,0:T(8,128)S(1)}, f32[1,16,512]{2,1,0:T(8,128)S(1)}, u32[]{:S(2)}, u32[]{:S(2)}) collective-permute-start(f32[1,16,512]{2,1,0:T(8,128)S(1)} %slice.224), channel_id=1, source_target_pairs={{32,0},{64,32},{96,64},{128,96},{160,128},{192,160},{224,192},{256... | collective-permute-start | bytes 98312 | tf_op jit(solution)/shard_map/ppermute | solution.py:21
  16.3 17.1 %copy-start.1 = (f32[1,8,16,512]{3,2,1,0:T(8,128)}, f32[1,8,16,512]{3,2,1,0:T(8,128)S(1)}, u32[]{:S(2)}) copy-start(f32[1,8,16,512]{3,2,1,0:T(8,128)S(1)} %copy.40) | copy-start | bytes 786436
  19.8 20.2 %copy-start.5 = (f32[10,16,512]{2,1,0:T(8,128)}, f32[10,16,512]{2,1,0:T(8,128)S(1)}, u32[]{:S(2)}) copy-start(f32[10,16,512]{2,1,0:T(8,128)S(1)} %constant_dynamic-update-slice_fusion) | copy-start | bytes 983044
  20.5 23.8 %collective-permute-start.2 = (f32[10,1,512]{2,1,0:T(1,128)}, f32[10,1,512]{2,1,0:T(1,128)}, u32[]{:S(2)}, u32[]{:S(2)}) collective-permute-start(f32[10,1,512]{2,1,0:T(1,128)} %get-tuple-element.16), channel_id=1, source_target_pairs={{1,0},{2,1},{3,2},{4,3},{5,4},{6,5},{7,6},{8,7},{9,8},{10,9},{11,1... | collective-permute-start | bytes 61448 | tf_op jit(solution)/shard_map/ppermute | solution.py:21
  31.4 12.9 %collective-permute-start.3 = (f32[10,1,512]{2,1,0:T(1,128)}, f32[10,1,512]{2,1,0:T(1,128)}, u32[]{:S(2)}, u32[]{:S(2)}) collective-permute-start(f32[10,1,512]{2,1,0:T(1,128)} %get-tuple-element.17), channel_id=1, source_target_pairs={{0,1},{1,2},{2,3},{3,4},{4,5},{5,6},{6,7},{7,8},{8,9},{9,10},{10,1... | collective-permute-start | bytes 61448 | tf_op jit(solution)/shard_map/ppermute | solution.py:18
  46.4 4.3 %collective-permute-start.4 = (f32[1,16,512]{2,1,0:T(8,128)S(1)}, f32[1,16,512]{2,1,0:T(8,128)S(1)}, u32[]{:S(2)}, u32[]{:S(2)}) collective-permute-start(f32[1,16,512]{2,1,0:T(8,128)S(1)} %get-tuple-element.31), channel_id=1, source_target_pairs={{32,0},{64,32},{96,64},{128,96},{160,128},{192,160},{224,192},{256... | collective-permute-start | bytes 98312 | tf_op jit(solution)/shard_map/ppermute | solution.py:21
  48.3 6.4 %collective-permute-start.5 = (f32[1,16,512]{2,1,0:T(8,128)S(1)}, f32[1,16,512]{2,1,0:T(8,128)S(1)}, u32[]{:S(2)}, u32[]{:S(2)}) collective-permute-start(f32[1,16,512]{2,1,0:T(8,128)S(1)} %get-tuple-element.30), channel_id=1, source_target_pairs={{0,32},{32,64},{64,96},{96,128},{128,160},{160,192},{192,224},{224... | collective-permute-start | bytes 98312 | tf_op jit(solution)/shard_map/ppermute | solution.py:18
  54.8 8.3 %collective-permute-start.6 = (f32[10,1,512]{2,1,0:T(1,128)S(1)}, f32[10,1,512]{2,1,0:T(1,128)S(1)}, u32[]{:S(2)}, u32[]{:S(2)}) collective-permute-start(f32[10,1,512]{2,1,0:T(1,128)S(1)} %get-tuple-element.14), channel_id=1, source_target_pairs={{1,0},{2,1},{3,2},{4,3},{5,4},{6,5},{7,6},{8,7},{9,8},{10,9},{11,1... | collective-permute-start | bytes 61448 | tf_op jit(solution)/shard_map/ppermute | solution.py:21
  60.8 7.8 %collective-permute-start.7 = (f32[10,1,512]{2,1,0:T(1,128)S(1)}, f32[10,1,512]{2,1,0:T(1,128)S(1)}, u32[]{:S(2)}, u32[]{:S(2)}) collective-permute-start(f32[10,1,512]{2,1,0:T(1,128)S(1)} %get-tuple-element.15), channel_id=1, source_target_pairs={{0,1},{1,2},{2,3},{3,4},{4,5},{5,6},{6,7},{7,8},{8,9},{9,10},{10,1... | collective-permute-start | bytes 61448 | tf_op jit(solution)/shard_map/ppermute | solution.py:18
  68.9 4.3 %collective-permute-start.8 = (f32[1,16,512]{2,1,0:T(8,128)S(1)}, f32[1,16,512]{2,1,0:T(8,128)S(1)}, u32[]{:S(2)}, u32[]{:S(2)}) collective-permute-start(f32[1,16,512]{2,1,0:T(8,128)S(1)} %get-tuple-element.27), channel_id=1, source_target_pairs={{32,0},{64,32},{96,64},{128,96},{160,128},{192,160},{224,192},{256... | collective-permute-start | bytes 98312 | tf_op jit(solution)/shard_map/ppermute | solution.py:21
  70.9 6.4 %collective-permute-start.9 = (f32[1,16,512]{2,1,0:T(8,128)S(1)}, f32[1,16,512]{2,1,0:T(8,128)S(1)}, u32[]{:S(2)}, u32[]{:S(2)}) collective-permute-start(f32[1,16,512]{2,1,0:T(8,128)S(1)} %get-tuple-element.26), channel_id=1, source_target_pairs={{0,32},{32,64},{64,96},{96,128},{128,160},{160,192},{192,224},{224... | collective-permute-start | bytes 98312 | tf_op jit(solution)/shard_map/ppermute | solution.py:18
  77.4 6.0 %collective-permute-start.10 = (f32[10,1,512]{2,1,0:T(1,128)S(1)}, f32[10,1,512]{2,1,0:T(1,128)S(1)}, u32[]{:S(2)}, u32[]{:S(2)}) collective-permute-start(f32[10,1,512]{2,1,0:T(1,128)S(1)} %get-tuple-element.12), channel_id=1, source_target_pairs={{1,0},{2,1},{3,2},{4,3},{5,4},{6,5},{7,6},{8,7},{9,8},{10,9},{11,1... | collective-permute-start | bytes 61448 | tf_op jit(solution)/shard_map/ppermute | solution.py:21
  79.3 7.8 %collective-permute-start.11 = (f32[10,1,512]{2,1,0:T(1,128)S(1)}, f32[10,1,512]{2,1,0:T(1,128)S(1)}, u32[]{:S(2)}, u32[]{:S(2)}) collective-permute-start(f32[10,1,512]{2,1,0:T(1,128)S(1)} %get-tuple-element.13), channel_id=1, source_target_pairs={{0,1},{1,2},{2,3},{3,4},{4,5},{5,6},{6,7},{7,8},{8,9},{9,10},{10,1... | collective-permute-start | bytes 61448 | tf_op jit(solution)/shard_map/ppermute | solution.py:18
  87.4 4.4 %collective-permute-start.12 = (f32[1,16,512]{2,1,0:T(8,128)S(1)}, f32[1,16,512]{2,1,0:T(8,128)S(1)}, u32[]{:S(2)}, u32[]{:S(2)}) collective-permute-start(f32[1,16,512]{2,1,0:T(8,128)S(1)} %get-tuple-element.23), channel_id=1, source_target_pairs={{32,0},{64,32},{96,64},{128,96},{160,128},{192,160},{224,192},{256... | collective-permute-start | bytes 98312 | tf_op jit(solution)/shard_map/ppermute | solution.py:21
  89.3 6.4 %collective-permute-start.13 = (f32[1,16,512]{2,1,0:T(8,128)S(1)}, f32[1,16,512]{2,1,0:T(8,128)S(1)}, u32[]{:S(2)}, u32[]{:S(2)}) collective-permute-start(f32[1,16,512]{2,1,0:T(8,128)S(1)} %get-tuple-element.22), channel_id=1, source_target_pairs={{0,32},{32,64},{64,96},{96,128},{128,160},{160,192},{192,224},{224... | collective-permute-start | bytes 98312 | tf_op jit(solution)/shard_map/ppermute | solution.py:18
  91.8 20.9 %copy-start.3 = (f32[512,128]{1,0:T(8,128)}, f32[512,128]{1,0:T(8,128)S(1)}, u32[]{:S(2)}) copy-start(f32[512,128]{1,0:T(8,128)S(1)} %reshape.154) | copy-start | bytes 786436
  91.8 20.9 %copy-start.2 = (f32[512,128]{1,0:T(8,128)}, f32[512,128]{1,0:T(8,128)S(1)}, u32[]{:S(2)}) copy-start(f32[512,128]{1,0:T(8,128)S(1)} %reshape.155) | copy-start | bytes 786436
  95.8 6.0 %collective-permute-start.14 = (f32[10,1,512]{2,1,0:T(1,128)S(1)}, f32[10,1,512]{2,1,0:T(1,128)S(1)}, u32[]{:S(2)}, u32[]{:S(2)}) collective-permute-start(f32[10,1,512]{2,1,0:T(1,128)S(1)} %get-tuple-element.10), channel_id=1, source_target_pairs={{1,0},{2,1},{3,2},{4,3},{5,4},{6,5},{7,6},{8,7},{9,8},{10,9},{11,1... | collective-permute-start | bytes 61448 | tf_op jit(solution)/shard_map/ppermute | solution.py:21
  97.8 7.8 %collective-permute-start.15 = (f32[10,1,512]{2,1,0:T(1,128)S(1)}, f32[10,1,512]{2,1,0:T(1,128)S(1)}, u32[]{:S(2)}, u32[]{:S(2)}) collective-permute-start(f32[10,1,512]{2,1,0:T(1,128)S(1)} %get-tuple-element.11), channel_id=1, source_target_pairs={{0,1},{1,2},{2,3},{3,4},{4,5},{5,6},{6,7},{7,8},{8,9},{9,10},{10,1... | collective-permute-start | bytes 61448 | tf_op jit(solution)/shard_map/ppermute | solution.py:18
  101.9 15.6 %copy-start.4 = (f32[512,128]{1,0:T(8,128)}, f32[512,128]{1,0:T(8,128)S(1)}, u32[]{:S(2)}) copy-start(f32[512,128]{1,0:T(8,128)S(1)} %reshape.156) | copy-start | bytes 786436
  253.8 16.9 %copy-start = (f32[8,8192]{1,0:T(8,128)S(1)}, f32[8,8192]{1,0:T(8,128)}, u32[]{:S(2)}) copy-start(f32[8,8192]{1,0:T(8,128)} %param.4) | copy-start | bytes 786436
  271.8 6.0 %collective-permute-start.16 = (f32[1,16,512]{2,1,0:T(8,128)S(1)}, f32[1,16,512]{2,1,0:T(8,128)S(1)}, u32[]{:S(2)}, u32[]{:S(2)}) collective-permute-start(f32[1,16,512]{2,1,0:T(8,128)S(1)} %get-tuple-element.19), channel_id=1, source_target_pairs={{32,0},{64,32},{96,64},{128,96},{160,128},{192,160},{224,192},{256... | collective-permute-start | bytes 98312 | tf_op jit(solution)/shard_map/ppermute | solution.py:21
  275.2 6.4 %collective-permute-start.17 = (f32[1,16,512]{2,1,0:T(8,128)S(1)}, f32[1,16,512]{2,1,0:T(8,128)S(1)}, u32[]{:S(2)}, u32[]{:S(2)}) collective-permute-start(f32[1,16,512]{2,1,0:T(8,128)S(1)} %get-tuple-element.18), channel_id=1, source_target_pairs={{0,32},{32,64},{64,96},{96,128},{128,160},{160,192},{192,224},{224... | collective-permute-start | bytes 98312 | tf_op jit(solution)/shard_map/ppermute | solution.py:18
  281.7 7.0 %collective-permute-start.18 = (f32[10,1,512]{2,1,0:T(1,128)S(1)}, f32[10,1,512]{2,1,0:T(1,128)S(1)}, u32[]{:S(2)}, u32[]{:S(2)}) collective-permute-start(f32[10,1,512]{2,1,0:T(1,128)S(1)} %get-tuple-element.8), channel_id=1, source_target_pairs={{1,0},{2,1},{3,2},{4,3},{5,4},{6,5},{7,6},{8,7},{9,8},{10,9},{11,1... | collective-permute-start | bytes 61448 | tf_op jit(solution)/shard_map/ppermute | solution.py:21
  286.6 7.8 %collective-permute-start.19 = (f32[10,1,512]{2,1,0:T(1,128)S(1)}, f32[10,1,512]{2,1,0:T(1,128)S(1)}, u32[]{:S(2)}, u32[]{:S(2)}) collective-permute-start(f32[10,1,512]{2,1,0:T(1,128)S(1)} %get-tuple-element.9), channel_id=1, source_target_pairs={{0,1},{1,2},{2,3},{3,4},{4,5},{5,6},{6,7},{7,8},{8,9},{9,10},{10,1... | collective-permute-start | bytes 61448 | tf_op jit(solution)/shard_map/ppermute | solution.py:18
Sparse Core Ops, SparseCore 0:
  118.3 128.4 all-gather.1
